TPU v7x, 256 devices: a whole 4x4x8 slice. The times are simulated.
256 devices in a mesh: row: 32 (over z, x), col: 8 (over y, core).
Axes of the slice: x: 4, y: 4, z: 8, core: 2. Of those that a mesh axis runs over, the one named last changes fastest.
Arguments:
- tokens: bfloat16 [1024, 8192], P('row', 'col'), may hold values from -6 to 6
- cotangent: bfloat16 [1024, 8192], P('row', 'col'), may hold values from -6 to 6
- gate_weight: bfloat16 [8192, 16384], P('col', 'row'), may hold values from -0.125 to 0.125
- up_weight: bfloat16 [8192, 16384], P('col', 'row'), may hold values from -0.125 to 0.125
- down_weight: bfloat16 [16384, 8192], P('row', 'col'), may hold values from -0.078125 to 0.078125
- gate_mask: int32 [64, 128], P('col', 'row'), may hold values 0 or 1
- up_mask: int32 [64, 128], P('col', 'row'), may hold values 0 or 1
- down_mask: int32 [128, 64], P('row', 'col'), may hold values 0 or 1
Outputs:
- layer_out: bfloat16 [1024, 8192], P('row', 'col')
- grad_tokens: bfloat16 [1024, 8192], P('row', 'col')
- grad_gate_weight: float32 [8192, 16384], P('col', 'row')
- grad_up_weight: float32 [8192, 16384], P('col', 'row')
- grad_down_weight: float32 [16384, 8192], P('row', 'col')
All inputs are finite; a program needn't handle non-finite values. No bound on the sum of `gate_mask` or of `up_mask` or of `down_mask` on one device may be relied on, other than what follows from the above.
Results may differ from a plain program's by a relative error of at most 0.0049.
Values may be sent and summed in bfloat16 or wider, within the bound.
No kernel may reach another device: no remote copies, remote signals or barrier semaphores. Data moves between devices by JAX's collectives and lax.ppermute only.
A program may use at most 128 MiB of HBM per device.

v0:
```python
import jax
import jax.numpy as jnp
from jax import lax
from jax.sharding import PartitionSpec as P

BLOCK = 128
contract_inner = (((1,), (1,)), ((), ()))
contract_outer = (((0,), (0,)), ((), ()))


def apply_pattern(weight, pattern):
    row_blocks, col_blocks = pattern.shape
    block_scale = pattern.astype(weight.dtype)
    blocks = weight.reshape(row_blocks, BLOCK, col_blocks, BLOCK) * block_scale[:, None, :, None]
    return blocks.reshape(weight.shape)


def col_reduce(summands, finish):
    summed = lax.psum(summands, "col")
    return finish(summed)


def shards(tokens, cotangent, gate_weight, up_weight, down_weight, gate_mask, up_mask, down_mask):
    hidden_width = gate_weight.shape[1]
    gathered_tokens, gathered_grads = (
        lax.all_gather(tokens, "row", axis=0, tiled=True),
        lax.all_gather(cotangent, "row", axis=0, tiled=True),
    )
    joint_weight = jnp.concatenate(
        [apply_pattern(gate_weight, gate_mask), apply_pattern(up_weight, up_mask)], axis=1
    )
    masked_down = apply_pattern(down_weight, down_mask)
    joint_part = jnp.dot(gathered_tokens, joint_weight, preferred_element_type=jnp.float32)

    def activate(joint_pre):
        gate_pre = joint_pre[:, :hidden_width]
        up_pre = joint_pre[:, hidden_width:]
        hidden_rows = (gate_pre * jax.nn.sigmoid(gate_pre) * up_pre).astype(jnp.bfloat16)
        return (hidden_rows, joint_pre)

    hidden, joint_pre = col_reduce(joint_part, activate)
    hidden_part = lax.dot_general(
        gathered_grads, masked_down, contract_inner, preferred_element_type=jnp.float32
    )

    def derive(grad_hidden):
        gate_pre = joint_pre[:, :hidden_width]
        up_pre = joint_pre[:, hidden_width:]
        sigmoid_gate = jax.nn.sigmoid(gate_pre)
        silu_gate = gate_pre * sigmoid_gate
        grad_gate_pre = (
            grad_hidden * up_pre * sigmoid_gate * (1.0 + gate_pre * (1.0 - sigmoid_gate))
        )
        grad_up_pre = grad_hidden * silu_gate
        joint_rows = jnp.concatenate(
            [grad_gate_pre.astype(jnp.bfloat16), grad_up_pre.astype(jnp.bfloat16)], axis=1
        )
        return (joint_rows, grad_hidden)

    joint_grad, unused = col_reduce(hidden_part, derive)
    output_term = jnp.dot(hidden, masked_down, preferred_element_type=jnp.float32)
    token_term = lax.dot_general(
        joint_grad, joint_weight, contract_inner, preferred_element_type=jnp.float32
    )
    layer_out, grad_tokens = (
        lax.psum_scatter(output_term, "row", scatter_dimension=0, tiled=True),
        lax.psum_scatter(token_term, "row", scatter_dimension=0, tiled=True),
    )
    weight_grads = lax.dot_general(
        gathered_tokens, joint_grad, contract_outer, preferred_element_type=jnp.float32
    )
    grad_gate_weight = apply_pattern(weight_grads[:, :hidden_width], gate_mask)
    grad_up_weight = apply_pattern(weight_grads[:, hidden_width:], up_mask)
    grad_down_weight = apply_pattern(
        lax.dot_general(hidden, gathered_grads, contract_outer, preferred_element_type=jnp.float32),
        down_mask,
    )
    return (
        layer_out.astype(jnp.bfloat16),
        grad_tokens.astype(jnp.bfloat16),
        grad_gate_weight,
        grad_up_weight,
        grad_down_weight,
    )


def solution(mesh):
    in_specs = (
        P("row", "col"),
        P("row", "col"),
        P("col", "row"),
        P("col", "row"),
        P("row", "col"),
        P("col", "row"),
        P("col", "row"),
        P("row", "col"),
    )
    out_specs = (
        P("row", "col"),
        P("row", "col"),
        P("col", "row"),
        P("col", "row"),
        P("row", "col"),
    )
    return jax.shard_map(shards, mesh=mesh, in_specs=in_specs, out_specs=out_specs, check_vma=False)
```

profile of v0, /device:TPU:8, one launch (start us, length us, event | category | flops | bytes accessed | tf_op | source)
XLA Modules:
  0.0 727.5 jit_solution(3877633077299212398)
XLA Ops:
  7.2 0.7 all-gather.3.cloned.1.call-update
  8.0 0.7 all-gather.5.cloned.1.call-update
  8.7 0.8 fusion.8
  9.6 0.8 fusion.7
  10.4 0.8 fusion.6
  11.2 0.3 mul.88
  11.5 0.3 mul.91
  11.9 1.3 bitcast_multiply_fusion.4
  13.2 78.2 %all-gather.3.cloned.1.call-done = bf16[1024,1024]{1,0:T(8,128)(2,1)} async-done(((bf16[32,1024]{1,0:T(8,128)(2,1)}), bf16[1024,1024]{1,0:T(8,128)(2,1)}) %all-gather.3.cloned.1.call-update) | async-done | bytes 2097168 | tf_op jit(solution)/shard_map/all_gather | solution.py:26
  91.4 6.4 convolution_bitcast_fusion.1
  97.8 71.4 %all-gather.5.cloned.1.call-done = bf16[1024,1024]{1,0:T(8,128)(2,1)} async-done(((bf16[32,1024]{1,0:T(8,128)(2,1)}), bf16[1024,1024]{1,0:T(8,128)(2,1)}) %all-gather.5.cloned.1.call-update) | async-done | bytes 2097168 | tf_op jit(solution)/shard_map/all_gather | solution.py:27
  169.2 0.2 mul.96
  169.4 4.2 convolution_bitcast_fusion.2
  173.7 84.3 %all-reduce.3.cloned.1.call-done = (f32[1024,1024]{0,1:T(8,128)}, f32[1024,512]{0,1:T(8,128)}) async-done(((f32[1024,1024]{0,1:T(8,128)}, f32[1024,512]{0,1:T(8,128)}), (f32[1024,1024]{0,1:T(8,128)}, f32[1024,512]{0,1:T(8,128)})) %all-reduce.3.cloned.1.call-update) | async-done | bytes 6291472 | tf_op jit(solution)/shard_map/psum | solution.py:19
  258.0 4.4 multiply_convert_fusion.1
  262.4 1.0 copy-done.1
  263.4 0.3 copy-done.3
  263.7 4.4 fusion.1
  268.1 0.2 reduce-scatter.3.cloned.1.call-start
  268.3 3.3 fusion.2
  271.6 1.2 copy-done.2
  272.8 0.3 copy-done.4
  273.1 3.9 convolution_bitcast_fusion
  277.4 2.8 bitcast_multiply_fusion.1
  280.3 2.9 copy.15
  283.2 1.8 copy.16
  285.2 1.4 copy-done.10
  286.6 2.7 bitcast_multiply_fusion
  289.3 204.7 %reduce-scatter.5.cloned.1.call-done = f32[32,1024]{1,0:T(8,128)} async-done(((f32[1024,1024]{1,0:T(8,128)}), f32[32,1024]{1,0:T(8,128)}) %reduce-scatter.5.cloned.1.call-update) | async-done | bytes 131088 | tf_op jit(solution)/shard_map/reduce_scatter | solution.py:67
  494.0 1.5 convert_element_type.40
  495.5 223.9 %reduce-scatter.3.cloned.1.call-done = f32[32,1024]{1,0:T(8,128)} async-done(((f32[1024,1024]{1,0:T(8,128)}), f32[32,1024]{1,0:T(8,128)}) %reduce-scatter.3.cloned.1.call-update) | async-done | bytes 131088 | tf_op jit(solution)/shard_map/reduce_scatter | solution.py:66
  719.5 1.5 convert_element_type.37
  (29 shorter events, 1.0 us)
Async XLA Ops:
  7.2 4.7 copy-start.6
  7.2 4.7 copy-start.5
  7.2 84.2 %all-gather.3.cloned.1.call-start = ((), (), s32[]{:S(2)}) async-start(), calls=%async_computation.2 | async-start | bytes 2162688 | tf_op jit(solution)/shard_map/all_gather | solution.py:26
  7.9 161.2 %all-gather.5.cloned.1.call-start = ((), (), s32[]{:S(2)}) async-start(), calls=%async_computation.4 | async-start | bytes 2162688 | tf_op jit(solution)/shard_map/all_gather | solution.py:27
  8.7 249.3 %all-reduce.3.cloned.1.call-start = ((), (), s32[]{:S(2)}) async-start(), calls=%async_computation.6 | async-start | bytes 12582912 | tf_op jit(solution)/shard_map/psum | solution.py:19
  13.2 84.6 %copy-start.7 = (bf16[1024,512]{1,0:T(8,128)(2,1)}, bf16[1024,512]{1,0:T(8,128)(2,1)S(1)}, u32[]{:S(2)}) copy-start(bf16[1024,512]{1,0:T(8,128)(2,1)S(1)} %get-tuple-element.23) | copy-start | bytes 3145732
  91.4 78.0 %copy-start = (bf16[512,1024]{1,0:T(8,128)(2,1)S(1)}, bf16[512,1024]{1,0:T(8,128)(2,1)}, u32[]{:S(2)}) copy-start(bf16[512,1024]{1,0:T(8,128)(2,1)} %param.12) | copy-start | bytes 3145732
  173.6 320.4 %reduce-scatter.5.cloned.1.call-start = ((), (), s32[]{:S(2)}) async-start(), calls=%async_computation.5 | async-start | bytes 4325376 | tf_op jit(solution)/shard_map/reduce_scatter | solution.py:67
  258.0 5.7 copy-start.8
  258.0 5.7 copy-start.9
  262.3 1.0 copy-start.1
  262.4 1.3 copy-start.3
  268.1 451.4 %reduce-scatter.3.cloned.1.call-start = ((), (), s32[]{:S(2)}) async-start(), calls=%async_computation.3 | async-start | bytes 4325376 | tf_op jit(solution)/shard_map/reduce_scatter | solution.py:66
  271.6 1.2 copy-start.2
  271.6 1.5 copy-start.4
  285.0 1.6 copy-start.10
Sparse Core Ops, SparseCore 0:
  10.6 80.7 all-gather.2
  94.0 75.1 all-gather.4
  173.7 84.1 all-reduce.2
  268.2 225.7 reduce-scatter.4
  497.7 221.6 reduce-scatter.2
where the time goes:
time: 728 us
  waiting for transfers between devices  664 us (91%)
  matrix products  24.9 us (3%)
  other arithmetic  13.9 us (2%)
  between operations  13.9 us (2%)
  local copies, waits for them, and re-layouts  10.6 us (1%)
    reduce_scatter x1, waiting for transfers between devices, shards(): lax.psum_scatter(output_term, 'row', scatter_dimension=0, tiled=True)  224 us
    reduce_scatter x1, waiting for transfers between devices, shards(): lax.psum_scatter(token_term, 'row', scatter_dimension=0, tiled=True)  205 us
    psum x1, waiting for transfers between devices, col_reduce(): summed = lax.psum(summands, 'col')  84.3 us
    all_gather x1, waiting for transfers between devices, shards(): lax.all_gather(tokens, 'row', axis=0, tiled=True)  78.2 us
    all_gather x1, waiting for transfers between devices, shards(): lax.all_gather(cotangent, 'row', axis=0, tiled=True)  71.4 us
  transfers between devices with their start and end apart: 5, of which 5 were waited for; matrix products, arithmetic and copies ran while one was open for 4% of the time, Pallas kernels for 0%

commit v1 on v0

--- a/solution.py
+++ b/solution.py
@@ -16,7 +16,7 @@
 
 
 def col_reduce(summands, finish):
-    summed = lax.psum(summands, "col")
+    summed = lax.all_gather(summands, axis_name="col").sum(axis=0)
     return finish(summed)
 
 

time: 728 us -> 934 us (1.28)
  waiting for transfers between devices: 664 us -> 794 us
  local copies, waits for them, and re-layouts: 10.6 us -> 68.2 us
  other arithmetic: 13.9 us -> 31.6 us
    all_gather x0 -> x2, waiting for transfers between devices: none -> 215 us  [col_reduce(): summed = lax.all_gather(summands, axis_name='col').sum(axis=0)]
    psum x1 -> x0, waiting for transfers between devices: 84.3 us -> none  [col_reduce(): summed = lax.psum(summands, 'col')]
    unnamed x24 -> x34, local copies, waits for them, and re-layouts: 8.91 us -> 66.5 us
    reduce_sum x0 -> x2, other arithmetic: none -> 19.2 us  [col_reduce(): summed = lax.all_gather(summands, axis_name='col').sum(axis=0)]
    all_gather x1, waiting for transfers between devices: 71.4 us -> 81.9 us  [shards(): lax.all_gather(cotangent, 'row', axis=0, tiled=True)]
  transfers between devices with their start and end apart: 5 -> 6, of which waited for: 5 -> 6; matrix products, arithmetic and copies ran while one was open for 4% -> 6% of each run, Pallas kernels for 0% -> 0%
where the time goes in v1:
time: 934 us; the launch traced here: 933 us
  waiting for transfers between devices  794 us (85%)
  local copies, waits for them, and re-layouts  68.2 us (7%)
  other arithmetic  31.6 us (3%)
  matrix products  25.2 us (3%)
  between operations  14.2 us (2%)
    reduce_scatter x1, waiting for transfers between devices, shards(): lax.psum_scatter(output_term, 'row', scatter_dimension=0, tiled=True)  224 us
    all_gather x2, waiting for transfers between devices, col_reduce(): summed = lax.all_gather(summands, axis_name='col').sum(axis=0)  215 us
    reduce_scatter x1, waiting for transfers between devices, shards(): lax.psum_scatter(token_term, 'row', scatter_dimension=0, tiled=True)  202 us
    all_gather x1, waiting for transfers between devices, shards(): lax.all_gather(cotangent, 'row', axis=0, tiled=True)  81.9 us
    all_gather x1, waiting for transfers between devices, shards(): lax.all_gather(tokens, 'row', axis=0, tiled=True)  69.2 us
    unnamed x34, local copies, waits for them, and re-layouts  66.5 us
    reduce_sum x2, other arithmetic, col_reduce(): summed = lax.all_gather(summands, axis_name='col').sum(axis=0)  19.2 us
  transfers between devices with their start and end apart: 6, of which 6 were waited for; matrix products, arithmetic and copies ran while one was open for 6% of the time, Pallas kernels for 0%

profile of v1, /device:TPU:8, one launch (start us, length us, event | category | flops | bytes accessed | tf_op | source)
XLA Modules:
  0.0 933.4 jit_solution(16355615271312193441)
XLA Ops:
  7.2 0.7 all-gather.9.cloned.1.call-update
  7.9 0.7 all-gather.7.cloned.1.call-update
  8.7 0.8 fusion.6
  9.5 81.9 %all-gather.9.cloned.1.call-done = bf16[1024,1024]{1,0:T(8,128)(2,1)} async-done(((bf16[32,1024]{1,0:T(8,128)(2,1)}), bf16[1024,1024]{1,0:T(8,128)(2,1)}) %all-gather.9.cloned.1.call-update) | async-done | bytes 2097168 | tf_op jit(solution)/shard_map/all_gather | solution.py:27
  91.6 1.0 copy-done
  92.6 4.5 convolution_bitcast_fusion.2
  97.2 0.6 copy-done.12
  98.7 1.3 bitcast_multiply_fusion.4
  100.0 69.2 %all-gather.7.cloned.1.call-done = bf16[1024,1024]{1,0:T(8,128)(2,1)} async-done(((bf16[32,1024]{1,0:T(8,128)(2,1)}), bf16[1024,1024]{1,0:T(8,128)(2,1)}) %all-gather.7.cloned.1.call-update) | async-done | bytes 2097168 | tf_op jit(solution)/shard_map/all_gather | solution.py:26
  169.1 6.4 convolution_bitcast_fusion.1
  175.8 80.1 %all-gather.13.cloned.1.call-done = f32[8192,512]{0,1:T(8,128)} async-done(((f32[1024,512]{0,1:T(8,128)}), f32[8192,512]{0,1:T(8,128)}) %all-gather.13.cloned.1.call-update) | async-done | bytes 16777232 | tf_op jit(solution)/shard_map/all_gather | solution.py:19
  255.9 19.7 %copy.25 = f32[64,8,8,1024]{3,2,1,0:T(8,128)S(1)} copy(f32[64,8,8,1024]{3,1,2,0:T(8,128)} %bitcast.53) | data formatting | bytes 33554432
  275.6 6.6 bitcast_reduce_fusion.1
  282.2 134.8 %all-gather.11.cloned.1.call-done = f32[8192,1024]{0,1:T(8,128)} async-done(((f32[1024,1024]{0,1:T(8,128)}), f32[8192,1024]{0,1:T(8,128)}) %all-gather.11.cloned.1.call-update) | async-done | bytes 33554448 | tf_op jit(solution)/shard_map/all_gather | solution.py:19
  417.1 34.9 %copy.23 = f32[128,8,8,1024]{3,2,1,0:T(8,128)S(1)} copy(f32[128,8,8,1024]{3,1,2,0:T(8,128)} %bitcast.52) | data formatting | bytes 67108864
  452.0 12.6 %bitcast_reduce_fusion = f32[1024,1024]{0,1:T(8,128)} fusion(f32[128,8,8,1024]{3,2,1,0:T(8,128)S(1)} %copy.23), kind=kLoop, calls=%fused_computation | loop fusion | flops 7340032 | bytes 37748736 | tf_op jit(solution)/shard_map/reduce_sum | solution.py:19
  464.5 4.4 multiply_convert_fusion.1
  468.9 1.0 copy-done.3
  470.2 4.4 fusion.1
  474.7 1.1 copy-done.1
  476.2 3.2 fusion.2
  479.5 1.2 copy-done.4
  481.0 3.9 convolution_bitcast_fusion
  485.3 2.8 bitcast_multiply_fusion.1
  488.2 2.9 copy.19
  491.0 1.8 copy.20
  493.1 1.4 copy-done.14
  494.5 2.7 bitcast_multiply_fusion
  497.2 202.2 %reduce-scatter.5.cloned.1.call-done = f32[32,1024]{1,0:T(8,128)} async-done(((f32[1024,1024]{1,0:T(8,128)}), f32[32,1024]{1,0:T(8,128)}) %reduce-scatter.5.cloned.1.call-update) | async-done | bytes 131088 | tf_op jit(solution)/shard_map/reduce_scatter | solution.py:67
  699.4 1.5 convert_element_type.40
  701.0 224.1 %reduce-scatter.3.cloned.1.call-done = f32[32,1024]{1,0:T(8,128)} async-done(((f32[1024,1024]{1,0:T(8,128)}), f32[32,1024]{1,0:T(8,128)}) %reduce-scatter.3.cloned.1.call-update) | async-done | bytes 131088 | tf_op jit(solution)/shard_map/reduce_scatter | solution.py:66
  925.0 1.5 convert_element_type.37
  (44 shorter events, 3.1 us)
Async XLA Ops:
  7.2 84.2 %all-gather.9.cloned.1.call-start = ((), (), s32[]{:S(2)}) async-start(), calls=%async_computation.4 | async-start | bytes 2162688 | tf_op jit(solution)/shard_map/all_gather | solution.py:27
  7.9 161.2 %all-gather.7.cloned.1.call-start = ((), (), s32[]{:S(2)}) async-start(), calls=%async_computation.2 | async-start | bytes 2162688 | tf_op jit(solution)/shard_map/all_gather | solution.py:26
  8.6 247.3 %all-gather.13.cloned.1.call-start = ((), (), s32[]{:S(2)}) async-start(), calls=%async_computation.7 | async-start | bytes 18874368 | tf_op jit(solution)/shard_map/all_gather | solution.py:19
  91.6 1.0 copy-start
  97.1 0.7 copy-start.12
  97.1 0.8 copy-start.13
  97.1 1.6 copy-start.7
  97.1 1.6 copy-start.8
  97.1 319.9 %all-gather.11.cloned.1.call-start = ((), (), s32[]{:S(2)}) async-start(), calls=%async_computation.6 | async-start | bytes 37748736 | tf_op jit(solution)/shard_map/all_gather | solution.py:19
  100.0 75.5 %copy-start.9 = (bf16[1024,512]{1,0:T(8,128)(2,1)}, bf16[1024,512]{1,0:T(8,128)(2,1)S(1)}, u32[]{:S(2)}) copy-start(bf16[1024,512]{1,0:T(8,128)(2,1)S(1)} %get-tuple-element.26) | copy-start | bytes 3145732
  175.5 523.9 %reduce-scatter.5.cloned.1.call-start = ((), (), s32[]{:S(2)}) async-start(), calls=%async_computation.5 | async-start | bytes 4325376 | tf_op jit(solution)/shard_map/reduce_scatter | solution.py:67
  464.5 5.7 copy-start.10
  464.5 5.7 copy-start.11
  468.9 1.1 copy-start.3
  468.9 1.3 copy-start.5
  474.6 1.2 copy-start.1
  474.6 1.5 copy-start.2
  474.7 450.3 %reduce-scatter.3.cloned.1.call-start = ((), (), s32[]{:S(2)}) async-start(), calls=%async_computation.3 | async-start | bytes 4325376 | tf_op jit(solution)/shard_map/reduce_scatter | solution.py:66
  479.4 1.2 copy-start.4
  479.4 1.5 copy-start.6
  492.9 1.6 copy-start.14
Sparse Core Ops, SparseCore 0:
  10.6 80.7 all-gather.8
  94.0 75.1 all-gather.6
  171.6 84.3 all-gather.12
  257.6 159.4 all-gather.10
  474.8 224.5 reduce-scatter.4
  703.2 221.8 reduce-scatter.2
